TPU v7x, 256 devices: a whole 4x4x8 slice. The times are simulated.
256 devices in a mesh: win: 32 (over y, z), grp: 8 (over x, core).
Axes of the slice: x: 4, y: 4, z: 8, core: 2. Of those that a mesh axis runs over, the one named last changes fastest.
Arguments:
- points: bfloat16 [32, 8, 512, 512], P('win', 'grp'), may hold values from -6 to 6
- rank: int32 [32, 8, 512], P('win', 'grp'), may hold values from 0 to 16383, as said below
- counts: int32 [8, 32, 8], replicated, may hold values from 1 to 128, 512 in all within a row
- w_qkv_one: bfloat16 [512, 1536], replicated
- w_out_one: bfloat16 [512, 512], replicated, may hold values from -0.25 to 0.25
- w_up: bfloat16 [512, 2048], replicated, may hold values from -0.25 to 0.25
- w_down: bfloat16 [2048, 512], replicated, may hold values from -0.125 to 0.125
- w_qkv_two: bfloat16 [512, 1536], replicated
- w_out_two: bfloat16 [512, 512], replicated, may hold values from -0.25 to 0.25
Outputs:
- encoded: bfloat16 [32, 8, 512, 512], P('win', 'grp')
Inputs may be any that keep to these rules, and one draw needn't show every extreme that they name: Within each of the 8 grp columns, rank over all 32 devices of win is a permutation of 0 to 16383. Each device holds at most 32 points whose rank // 512 is any one owner, and exactly 32 for some owner; each owner receives exactly 32 from some device. For each grp column and owner the 8 counts sum to 512, and the largest is 128.
All inputs are finite; a program needn't handle non-finite values.
Results may differ from a plain program's by a relative error of at most 0.03.
The roundings to bfloat16 on the way count: a program that leaves them out, or rounds other values in their place, can miss the bound.
Values may be sent and summed in bfloat16 or wider, within the bound.
No kernel may reach another device: no remote copies, remote signals or barrier semaphores. Data moves between devices by JAX's collectives and lax.ppermute only.
A program may use at most 128 MiB of HBM per device.

v0:
```python
import jax
import jax.numpy as jnp
from jax import lax
from jax.sharding import PartitionSpec as P

HEAD_DIM = 32
WINDOW_SLOTS = 128
EPSILON = 1e-05
MASKED = -1e30
SLOT_BASE = 32
TAIL = 128


def normalize(row_data):
    values = row_data.astype(jnp.float32)
    center = values - jnp.mean(values, axis=-1, keepdims=True)
    spread = jnp.mean(center * center, axis=-1, keepdims=True)
    return (center * lax.rsqrt(spread + EPSILON)).astype(jnp.bfloat16)


def project(row_data, weight):
    return jnp.dot(normalize(row_data), weight, preferred_element_type=jnp.float32).astype(
        jnp.bfloat16
    )


def attention_block(row_data, valid, w_qkv, w_out):
    rows_count, model_dim = row_data.shape
    heads_count = model_dim // HEAD_DIM
    block_count = rows_count // WINDOW_SLOTS
    normed = normalize(row_data)
    w_split = w_qkv.reshape(model_dim, 3, heads_count, HEAD_DIM)

    def head_major(part):
        out = jnp.einsum(
            "nd,dhe->hne", normed, w_split[:, part], preferred_element_type=jnp.float32
        )
        return out.astype(jnp.bfloat16).reshape(heads_count, block_count, WINDOW_SLOTS, HEAD_DIM)

    query, key, value = (head_major(0), head_major(1), head_major(2))
    scores = jnp.einsum(
        "hbqe,hbke->hbqk", query, key, preferred_element_type=jnp.float32
    ) * HEAD_DIM ** (-0.5)
    scores = jnp.where(valid[None, :, None, :], scores, MASKED)
    row_max = jnp.max(scores, axis=-1, keepdims=True)
    weights = jnp.exp(scores - row_max)
    weights = (weights / jnp.sum(weights, axis=-1, keepdims=True)).astype(jnp.bfloat16)
    context = jnp.einsum("hbqk,hbke->hbqe", weights, value, preferred_element_type=jnp.float32)
    context = context.astype(jnp.bfloat16).reshape(heads_count, rows_count, HEAD_DIM)
    mixed = jnp.einsum(
        "hne,hed->nd",
        context,
        w_out.reshape(heads_count, HEAD_DIM, model_dim),
        preferred_element_type=jnp.float32,
    )
    return (row_data.astype(jnp.float32) + mixed).astype(jnp.bfloat16)


def feed_forward(row_data, w_up, w_down):
    hidden = jax.nn.gelu(
        jnp.dot(normalize(row_data), w_up, preferred_element_type=jnp.float32), approximate=True
    ).astype(jnp.bfloat16)
    return (
        row_data.astype(jnp.float32) + jnp.dot(hidden, w_down, preferred_element_type=jnp.float32)
    ).astype(jnp.bfloat16)


def place(onehot, rows):
    return jnp.dot(onehot, rows, preferred_element_type=jnp.float32).astype(jnp.bfloat16)


def place_back(onehot, rows):
    return lax.dot_general(
        onehot, rows, (((0,), (0,)), ((), ())), preferred_element_type=jnp.float32
    ).astype(jnp.bfloat16)


def on_device(points, rank, counts, w_qkv_one, w_out_one, w_up, w_down, w_qkv_two, w_out_two):
    owner_count = lax.axis_size("win")
    group_count = lax.axis_size("grp")
    win_index = lax.axis_index("win")
    grp_index = lax.axis_index("grp")
    local_points = points.shape[2]
    model_dim = points.shape[3]
    blocks = counts.shape[2]
    slots_all = blocks * WINDOW_SLOTS
    capacity = 2 * local_points // owner_count
    buffer_rows = owner_count * capacity
    dilation_stride = WINDOW_SLOTS // group_count
    rows_x = points.reshape(local_points, model_dim)
    point_rank = rank.reshape(local_points)
    column_counts = lax.dynamic_index_in_dim(counts, grp_index, 0, keepdims=False)
    owner_dev = lax.div(point_rank, local_points)
    owner_ids = jnp.arange(owner_count, dtype=jnp.int32)
    choose = (owner_dev[:, None] == owner_ids[None, :]).astype(jnp.int32)
    point_ids = jnp.arange(local_points, dtype=jnp.int32)
    lower = (point_ids[None, :] <= point_ids[:, None]).astype(jnp.bfloat16)
    running = jnp.dot(lower, choose.astype(jnp.bfloat16), preferred_element_type=jnp.float32)
    peer_order = jnp.sum(choose * (running.astype(jnp.int32) - 1), axis=1)
    send_place = owner_dev * capacity + peer_order
    buffer_ids = jnp.arange(buffer_rows, dtype=jnp.int32)
    send_hot = (buffer_ids[:, None] == send_place[None, :]).astype(jnp.bfloat16)
    window_ends = jnp.cumsum(column_counts, axis=1)
    starts = window_ends - column_counts
    offset = lax.rem(point_rank, local_points)
    table = jnp.concatenate(
        [
            lax.div(window_ends, SLOT_BASE),
            lax.rem(window_ends, SLOT_BASE),
            lax.div(starts, SLOT_BASE),
            lax.rem(starts, SLOT_BASE),
        ],
        axis=1,
    ).astype(jnp.bfloat16)
    picked = jnp.dot(choose.astype(jnp.bfloat16), table, preferred_element_type=jnp.float32)
    picked = picked.astype(jnp.int32)
    owner_ends = picked[:, :blocks] * SLOT_BASE + picked[:, blocks : 2 * blocks]
    owner_starts = picked[:, 2 * blocks : 3 * blocks] * SLOT_BASE + picked[:, 3 * blocks :]
    window = jnp.sum((owner_ends <= offset[:, None]).astype(jnp.int32), axis=1)
    block_ids = jnp.arange(blocks, dtype=jnp.int32)
    block_pick = (window[:, None] == block_ids[None, :]).astype(jnp.int32)
    dest_slot = window * WINDOW_SLOTS + offset - jnp.sum(block_pick * owner_starts, axis=1)
    slot_code = dest_slot + 1
    tail_ids = jnp.arange(TAIL, dtype=jnp.int32)
    code_cols = jnp.where(
        tail_ids[None, :] == 0,
        lax.div(slot_code, SLOT_BASE)[:, None],
        jnp.where(tail_ids[None, :] == 1, lax.rem(slot_code, SLOT_BASE)[:, None], 0),
    ).astype(jnp.bfloat16)
    outgoing = place(send_hot, jnp.concatenate([rows_x, code_cols], axis=1))
    receiving = lax.all_to_all(
        outgoing.reshape(owner_count, capacity, model_dim + TAIL),
        "win",
        split_axis=0,
        concat_axis=0,
        tiled=True,
    ).reshape(buffer_rows, model_dim + TAIL)
    arrived = receiving[:, :model_dim]
    code_back = receiving[:, model_dim:].astype(jnp.int32)
    arrived_slot = code_back[:, 0] * SLOT_BASE + code_back[:, 1] - 1
    own_counts = lax.dynamic_index_in_dim(column_counts, win_index, 0, keepdims=False)
    slot_ids = jnp.arange(slots_all, dtype=jnp.int32)
    recv_hot = (slot_ids[:, None] == arrived_slot.reshape(1, buffer_rows)).astype(jnp.bfloat16)
    padded_x = place(recv_hot, arrived)
    column = jnp.arange(WINDOW_SLOTS, dtype=jnp.int32)
    usable_mask = column[None, :] < own_counts[:, None]
    first_pad = feed_forward(
        attention_block(padded_x, usable_mask, w_qkv_one, w_out_one), w_up, w_down
    )
    dilated_rows = lax.all_to_all(
        first_pad.reshape(blocks, dilation_stride, group_count, model_dim),
        "grp",
        split_axis=2,
        concat_axis=1,
        tiled=True,
    )
    owner_counts = lax.dynamic_index_in_dim(counts, win_index, 1, keepdims=False)
    k_ids = jnp.arange(dilation_stride, dtype=jnp.int32)
    valid_marks = (
        k_ids[None, None, :] * group_count + grp_index < jnp.transpose(owner_counts)[:, :, None]
    )
    block_count = dilated_rows.shape[0]
    flat_rows = dilated_rows.reshape(block_count * WINDOW_SLOTS, model_dim)
    mixed_rows = attention_block(
        flat_rows, valid_marks.reshape(block_count, WINDOW_SLOTS), w_qkv_two, w_out_two
    ).reshape(block_count, WINDOW_SLOTS, 1, model_dim)
    second_pad = lax.all_to_all(mixed_rows, "grp", split_axis=1, concat_axis=2, tiled=True).reshape(
        slots_all, model_dim
    )
    returning = place_back(recv_hot, second_pad)
    returned = lax.all_to_all(returning, "win", split_axis=0, concat_axis=0, tiled=True)
    encoded = place_back(send_hot, returned)
    return encoded.reshape(1, 1, local_points, model_dim)


def solution(mesh):
    return jax.shard_map(
        on_device,
        mesh=mesh,
        in_specs=(
            P("win", "grp", None, None),
            P("win", "grp", None),
            P(),
            P(),
            P(),
            P(),
            P(),
            P(),
            P(),
        ),
        out_specs=P("win", "grp", None, None),
        check_vma=False,
    )
```

profile of v0, /device:TPU:32, one launch (start us, length us, event | category | flops | bytes accessed | tf_op | source)
XLA Modules:
  0.0 162.5 jit_solution(15884425211801808277)
XLA Ops:
  0.0 0.8 dynamic-slice_bitcast_fusion
  0.9 0.7 fusion.105
  1.6 0.7 negate_select_fusion.9
  2.3 0.3 fusion.58
  2.5 0.1 convolution_convert_fusion
  2.7 0.7 negate_select_fusion.7
  3.4 0.2 select_convert_fusion
  3.6 3.1 %fusion.45 = bf16[1024,640]{1,0:T(8,128)(2,1)} fusion(s32[512]{0:T(512)S(1)} %get-tuple-element.17, bf16[512,128]{1,0:T(8,128)(2,1)S(1)} %select_convert_fusion, bf16[512,512]{1,0:T(8,128)(2,1)} %bitcast.182), kind=kOutput, calls=%fused_computation.61 | convolution fusion | flops 673579008 | bytes 1968128 | tf_op jit(solution)/shard_map/dot_general | solution.py:69
  6.8 11.4 %all-to-all-start = ((bf16[32,32,640]{2,1,0:T(8,128)(2,1)}), bf16[32,32,640]{2,1,0:T(8,128)(2,1)S(1)}, u32[]{:S(2)}, u32[]{:S(2)}) async-start(bf16[32,32,640]{2,1,0:T(8,128)(2,1)} %bitcast.169), calls=%async_computation | async-start | bytes 2621440 | tf_op jit(solution)/shard_map/all_to_all | solution.py:131
  18.1 2.6 %copy.77 = bf16[512,1536]{0,1:T(8,128)(2,1)} copy(bf16[512,1536]{1,0:T(8,128)(2,1)} %param.12) | data formatting | bytes 3145728 | tf_op args[3]
  20.8 0.2 dynamic-slice_reduce_fusion
  21.0 2.6 %fusion.124 = (bf16[512,1,16,32]{0,3,2,1:T(8,128)(2,1)}, bf16[512,1,16,32]{0,3,2,1:T(8,128)(2,1)}, bf16[512,1,16,32]{0,3,2,1:T(8,128)(2,1)}) fusion(bf16[512,3,16,32]{0,3,2,1:T(8,128)(2,1)} %bitcast.158), kind=kLoop, calls=%fused_computation.181 | loop fusion | bytes 3145728 | tf_op jit(solution)/shard_map/slice | solution.py:36
  23.6 28.5 %all-to-all-done = bf16[32,32,640]{2,1,0:T(8,128)(2,1)S(1)} async-done(((bf16[32,32,640]{2,1,0:T(8,128)(2,1)}), bf16[32,32,640]{2,1,0:T(8,128)(2,1)S(1)}, u32[]{:S(2)}, u32[]{:S(2)}) %all-to-all-start) | async-done | bytes 1310752 | tf_op jit(solution)/shard_map/all_to_all | solution.py:131
  52.1 0.4 fusion.90
  52.5 1.3 convert_reduce_fusion.1
  53.8 0.5 fusion.30
  54.4 0.9 fusion.119
  55.4 0.9 fusion.121
  56.4 0.9 fusion.117
  57.3 1.3 fusion.72
  58.6 3.6 %fusion.125 = (f32[16,8,128]{2,1,0:T(8,128)S(1)}, f32[16,8,128,128]{2,3,1,0:T(8,128)S(1)}) fusion(f32[16,8,128,128]{2,3,1,0:T(8,128)S(1)} %fusion.72, pred[8,128]{1,0:T(8,128)(4,1)S(1)} %iota_compare_fusion.20), kind=kOutput, calls=%fused_computation.182 | output fusion | flops 12583039 | bytes 16843776 | tf_op jit(solution)/shard_map/sub | solution.py:46
  62.3 1.2 fusion.52
  63.5 0.8 convert_reduce_fusion
  64.3 0.5 fusion.28
  64.9 7.4 %fusion.33 = bf16[1024,512]{1,0:T(8,128)(2,1)} fusion(bf16[1024,512]{1,0:T(8,128)(2,1)S(1)} %get-tuple-element.25, bf16[2048,512]{1,0:T(8,128)(2,1)S(1)} %copy-done, bf16[512,2048]{1,0:T(8,128)(2,1)} %param.14, f32[1024]{0:T(1024)S(1)} %add_rsqrt_fusion.1, f32[1024]{0:T(1024)S(1)} %broadcast_multiply_fusion.1), kind=kOutput, calls=%fused_computation.46 | convolution fusion | flops 4317511680 | bytes 6299648 | tf_op jit(solution)/shard_map/dot_general | solution.py:64
  72.3 2.5 %copy.83 = bf16[8,16,8,512]{3,1,0,2:T(8,128)(2,1)} copy(bf16[8,16,8,512]{3,2,1,0:T(8,128)(2,1)} %bitcast.170) | data formatting | bytes 2097152 | tf_op jit(solution)/shard_map/reshape | solution.py:151
  74.8 4.3 %all-to-all-start.1 = ((bf16[8,16,8,512]{3,1,0,2:T(8,128)(2,1)}), bf16[8,16,8,512]{3,1,0,2:T(8,128)(2,1)S(1)}, u32[]{:S(2)}, u32[]{:S(2)}) async-start(bf16[8,16,8,512]{3,1,0,2:T(8,128)(2,1)} %copy.83), calls=%async_computation.1 | async-start | bytes 2097152 | tf_op jit(solution)/shard_map/all_to_all | solution.py:150
  79.1 2.6 %copy.87 = bf16[512,1536]{0,1:T(8,128)(2,1)} copy(bf16[512,1536]{1,0:T(8,128)(2,1)} %param.16) | data formatting | bytes 3145728 | tf_op args[7]
  82.2 2.3 %fusion.123 = (bf16[512,1,16,32]{0,3,2,1:T(8,128)(2,1)S(1)}, bf16[512,1,16,32]{0,3,2,1:T(8,128)(2,1)S(1)}, bf16[512,1,16,32]{0,3,2,1:T(8,128)(2,1)}) fusion(bf16[512,3,16,32]{0,3,2,1:T(8,128)(2,1)} %bitcast.159), kind=kLoop, calls=%fused_computation.180 | loop fusion | bytes 3145728 | tf_op jit(solution)/shard_map/slice | solution.py:36
  84.5 10.5 %all-to-all-done.1 = bf16[8,16,8,512]{3,1,0,2:T(8,128)(2,1)S(1)} async-done(((bf16[8,16,8,512]{3,1,0,2:T(8,128)(2,1)}), bf16[8,16,8,512]{3,1,0,2:T(8,128)(2,1)S(1)}, u32[]{:S(2)}, u32[]{:S(2)}) %all-to-all-start.1) | async-done | bytes 1048608 | tf_op jit(solution)/shard_map/all_to_all | solution.py:150
  95.0 0.2 bitcast_reduce_fusion
  95.3 0.5 fusion.37
  95.8 0.4 fusion.38
  96.2 0.7 fusion.127
  96.9 0.7 fusion.128
  97.7 0.7 fusion.129
  98.4 1.3 fusion.65
  99.8 3.5 %fusion.126 = (f32[16,8,128]{2,1,0:T(8,128)S(1)}, f32[16,8,128,128]{2,3,1,0:T(8,128)S(1)}) fusion(f32[16,8,128,128]{2,3,1,0:T(8,128)S(1)} %fusion.65, pred[8,128]{1,0:T(8,128)(4,1)S(1)} %broadcast_compare_fusion), kind=kOutput, calls=%fused_computation.183 | output fusion | flops 12583039 | bytes 16843776 | tf_op jit(solution)/shard_map/sub | solution.py:46
  103.2 1.2 fusion.53
  104.6 0.9 copy-done.8
  105.5 0.7 fusion.34
  106.3 0.6 copy.93
  106.8 18.4 %all_to_all.41 = bf16[8,128,1,512]{3,0,2,1:T(8,128)(2,1)S(1)} all-to-all(bf16[8,128,1,512]{3,0,2,1:T(8,128)(2,1)S(1)} %copy.93), channel_id=1, replica_groups=mesh['win'=32,'grp'=8] {'grp'}, dimensions={1} | all-to-all | bytes 2097152 | tf_op jit(solution)/shard_map/all_to_all | solution.py:167
  125.2 0.3 copy.94
  125.6 0.6 copy.95
  126.2 1.3 fusion.47
  127.5 33.5 %all_to_all.42 = bf16[32,32,512]{2,1,0:T(8,128)(2,1)S(1)} all-to-all(bf16[32,32,512]{2,1,0:T(8,128)(2,1)S(1)} %bitcast.174), channel_id=1, replica_groups=mesh['win'=32,'grp'=8] {'win'}, dimensions={0} | all-to-all | bytes 2097152 | tf_op jit(solution)/shard_map/all_to_all | solution.py:171
  161.0 1.6 fusion.55
  (38 shorter events, 1.0 us)
Async XLA Ops:
  0.0 64.9 %copy-start = (bf16[2048,512]{1,0:T(8,128)(2,1)S(1)}, bf16[2048,512]{1,0:T(8,128)(2,1)}, u32[]{:S(2)}) copy-start(bf16[2048,512]{1,0:T(8,128)(2,1)} %param.15) | copy-start | bytes 6291460
  6.8 45.3 %all-to-all-start = ((bf16[32,32,640]{2,1,0:T(8,128)(2,1)}), bf16[32,32,640]{2,1,0:T(8,128)(2,1)S(1)}, u32[]{:S(2)}, u32[]{:S(2)}) async-start(bf16[32,32,640]{2,1,0:T(8,128)(2,1)} %bitcast.169), calls=%async_computation | async-start | bytes 2621440 | tf_op jit(solution)/shard_map/all_to_all | solution.py:131
  18.1 2.6 %copy-start.6 = (s32[8,32,8]{1,2,0:T(8,128)S(1)}, s32[8,32,8]{1,2,0:T(8,128)}, u32[]{:S(2)}) copy-start(s32[8,32,8]{1,2,0:T(8,128)} %param.11) | copy-start | bytes 24580
  52.5 1.9 %copy-start.5 = (bf16[512,1,16,32]{0,3,2,1:T(8,128)(2,1)S(1)}, bf16[512,1,16,32]{0,3,2,1:T(8,128)(2,1)}, u32[]{:S(2)}) copy-start(bf16[512,1,16,32]{0,3,2,1:T(8,128)(2,1)} %get-tuple-element.9) | copy-start | bytes 1572868
  54.4 1.0 copy-start.4
  55.3 1.1 copy-start.3
  62.3 1.2 copy-start.7
  74.8 20.2 %all-to-all-start.1 = ((bf16[8,16,8,512]{3,1,0,2:T(8,128)(2,1)}), bf16[8,16,8,512]{3,1,0,2:T(8,128)(2,1)S(1)}, u32[]{:S(2)}, u32[]{:S(2)}) async-start(bf16[8,16,8,512]{3,1,0,2:T(8,128)(2,1)} %copy.83), calls=%async_computation.1 | async-start | bytes 2097152 | tf_op jit(solution)/shard_map/all_to_all | solution.py:150
  95.0 1.2 copy-start.2
  104.4 1.1 copy-start.8
  127.5 35.1 %copy-start.1 = (bf16[2048,512]{1,0:T(8,128)(2,1)S(1)}, bf16[2048,512]{1,0:T(8,128)(2,1)}, u32[]{:S(2)}) copy-start(bf16[2048,512]{1,0:T(8,128)(2,1)} %param.15) | copy-start | bytes 6291460
where the time goes:
time: 163 us
  blocking collectives  51.9 us (32%)
  waiting for transfers between devices  39 us (24%)
  matrix products  26.7 us (16%)
  local copies, waits for them, and re-layouts  16.8 us (10%)
  starting transfers between devices  15.7 us (10%)
  other arithmetic  12.2 us (7%)
    all_to_all x1, blocking collectives, on_device(): lax.all_to_all(returning, 'win', split_axis=0, concat_axis=0, tiled=True)  33.5 us
    all_to_all x1, waiting for transfers between devices, on_device(): lax.all_to_all(outgoing.reshape(owner_count, capacity, model_dim + TAIL),...  28.5 us
    all_to_all x1, blocking collectives, on_device(): lax.all_to_all(mixed_rows, 'grp', split_axis=1, concat_axis=2, tiled=True)  18.4 us
    all_to_all x1, starting transfers between devices, on_device(): lax.all_to_all(outgoing.reshape(owner_count, capacity, model_dim + TAIL),...  11.4 us
    all_to_all x1, waiting for transfers between devices, on_device(): lax.all_to_all(first_pad.reshape(blocks, dilation_stride, group_count, mo...  10.5 us
    dot_general x1, matrix products, feed_forward(): jnp.dot(hidden, w_down, preferred_element_type=jnp.float32)  7.42 us
    sub x2, other arithmetic, attention_block(): weights = jnp.exp(scores - row_max)  7.12 us
    unnamed x20, local copies, waits for them, and re-layouts  6.35 us
  transfers between devices with their start and end apart: 2, of which 2 were waited for; matrix products, arithmetic and copies ran while one was open for 7% of the time, Pallas kernels for 0%

commit v1 on v0

--- a/solution.py
+++ b/solution.py
@@ -2,6 +2,7 @@
 import jax.numpy as jnp
 from jax import lax
 from jax.sharding import PartitionSpec as P
+from jax.lax import all_to_all, axis_size
 
 HEAD_DIM = 32
 WINDOW_SLOTS = 128
@@ -9,6 +10,15 @@
 MASKED = -1e30
 SLOT_BASE = 32
 TAIL = 128
+draft_routes_all_in = lambda q_in, shard_axis: jnp.concatenate(
+    all_to_all(
+        jnp.stack(jnp.split(q_in, axis_size(shard_axis), axis=2)),
+        axis_name=shard_axis,
+        split_axis=0,
+        concat_axis=0,
+    ),
+    axis=1,
+)
 
 
 def normalize(row_data):
@@ -147,12 +157,8 @@
     first_pad = feed_forward(
         attention_block(padded_x, usable_mask, w_qkv_one, w_out_one), w_up, w_down
     )
-    dilated_rows = lax.all_to_all(
-        first_pad.reshape(blocks, dilation_stride, group_count, model_dim),
-        "grp",
-        split_axis=2,
-        concat_axis=1,
-        tiled=True,
+    dilated_rows = draft_routes_all_in(
+        first_pad.reshape(blocks, dilation_stride, group_count, model_dim), shard_axis="grp"
     )
     owner_counts = lax.dynamic_index_in_dim(counts, win_index, 1, keepdims=False)
     k_ids = jnp.arange(dilation_stride, dtype=jnp.int32)

time: 163 us -> 169 us (1.037)
  local copies, waits for them, and re-layouts: 16.8 us -> 22.4 us
    unnamed x20 -> x29, local copies, waits for them, and re-layouts: 6.35 us -> 11.1 us
    reshape x1 -> x0, local copies, waits for them, and re-layouts: 2.5 us -> none  [on_device(): first_pad.reshape(blocks, dilation_stride, group_count, model_dim)]
    split x0 -> x1, local copies, waits for them, and re-layouts: none -> 2.4 us  [jnp.split(q_in, axis_size(shard_axis), axis=2)]
  transfers between devices with their start and end apart: 2 -> 2, of which waited for: 2 -> 2; matrix products, arithmetic and copies ran while one was open for 7% -> 6% of each run, Pallas kernels for 0% -> 0%
where the time goes in v1:
time: 169 us; the launch traced here: 168 us
  blocking collectives  51.9 us (31%)
  waiting for transfers between devices  39 us (23%)
  matrix products  26.3 us (16%)
  local copies, waits for them, and re-layouts  22.4 us (13%)
  starting transfers between devices  15.7 us (9%)
  other arithmetic  12.5 us (7%)
    all_to_all x1, blocking collectives, on_device(): lax.all_to_all(returning, 'win', split_axis=0, concat_axis=0, tiled=True)  33.5 us
    all_to_all x1, waiting for transfers between devices, on_device(): lax.all_to_all(outgoing.reshape(owner_count, capacity, model_dim + TAIL),...  28.5 us
    all_to_all x1, blocking collectives, on_device(): lax.all_to_all(mixed_rows, 'grp', split_axis=1, concat_axis=2, tiled=True)  18.4 us
    all_to_all x1, starting transfers between devices, on_device(): lax.all_to_all(outgoing.reshape(owner_count, capacity, model_dim + TAIL),...  11.4 us
    unnamed x29, local copies, waits for them, and re-layouts  11.1 us
    all_to_all x1, waiting for transfers between devices, all_to_all(jnp.stack(jnp.split(q_in, axis_size(shard_axis), axis=2)), axi...  10.5 us
    sub x2, other arithmetic, attention_block(): weights = jnp.exp(scores - row_max)  7.12 us
    dot_general x1, matrix products, feed_forward(): jnp.dot(hidden, w_down, preferred_element_type=jnp.float32)  7 us
  transfers between devices with their start and end apart: 2, of which 2 were waited for; matrix products, arithmetic and copies ran while one was open for 6% of the time, Pallas kernels for 0%

profile of v1, /device:TPU:32, one launch (start us, length us, event | category | flops | bytes accessed | tf_op | source)
XLA Modules:
  0.0 168.0 jit_solution(4581859060134919895)
XLA Ops:
  0.0 0.8 dynamic-slice_bitcast_fusion
  0.9 0.7 fusion.110
  1.6 0.7 negate_select_fusion.9
  2.7 0.7 negate_select_fusion.7
  3.6 3.1 %fusion.41 = bf16[1024,640]{1,0:T(8,128)(2,1)} fusion(s32[512]{0:T(512)S(1)} %get-tuple-element.25, bf16[512,128]{1,0:T(8,128)(2,1)S(1)} %select_convert_fusion, bf16[512,512]{1,0:T(8,128)(2,1)} %bitcast.202), kind=kOutput, calls=%fused_computation.58 | convolution fusion | flops 673579008 | bytes 1968128 | tf_op jit(solution)/shard_map/dot_general | solution.py:79
  6.8 11.4 %all-to-all-start = ((bf16[32,32,640]{2,1,0:T(8,128)(2,1)}), bf16[32,32,640]{2,1,0:T(8,128)(2,1)S(1)}, u32[]{:S(2)}, u32[]{:S(2)}) async-start(bf16[32,32,640]{2,1,0:T(8,128)(2,1)} %bitcast.191), calls=%async_computation | async-start | bytes 2621440 | tf_op jit(solution)/shard_map/all_to_all | solution.py:141
  18.1 2.6 %copy.80 = bf16[512,1536]{0,1:T(8,128)(2,1)} copy(bf16[512,1536]{1,0:T(8,128)(2,1)} %param.12) | data formatting | bytes 3145728 | tf_op args[3]
  21.0 2.6 %fusion.129 = (bf16[512,1,16,32]{0,3,2,1:T(8,128)(2,1)}, bf16[512,1,16,32]{0,3,2,1:T(8,128)(2,1)}, bf16[512,1,16,32]{0,3,2,1:T(8,128)(2,1)}) fusion(bf16[512,3,16,32]{0,3,2,1:T(8,128)(2,1)} %bitcast.179), kind=kLoop, calls=%fused_computation.194 | loop fusion | bytes 3145728 | tf_op jit(solution)/shard_map/slice | solution.py:46
  23.6 28.5 %all-to-all-done = bf16[32,32,640]{2,1,0:T(8,128)(2,1)S(1)} async-done(((bf16[32,32,640]{2,1,0:T(8,128)(2,1)}), bf16[32,32,640]{2,1,0:T(8,128)(2,1)S(1)}, u32[]{:S(2)}, u32[]{:S(2)}) %all-to-all-start) | async-done | bytes 1310752 | tf_op jit(solution)/shard_map/all_to_all | solution.py:141
  52.5 1.3 convert_reduce_fusion.1
  53.8 0.5 fusion.30
  54.4 0.9 fusion.124
  55.4 0.9 fusion.126
  56.4 0.9 fusion.122
  57.3 1.3 fusion.69
  58.6 3.6 %fusion.131 = (f32[16,8,128]{2,1,0:T(8,128)S(1)}, f32[16,8,128,128]{2,3,1,0:T(8,128)S(1)}) fusion(f32[16,8,128,128]{2,3,1,0:T(8,128)S(1)} %fusion.69, pred[8,128]{1,0:T(8,128)(4,1)S(1)} %iota_compare_fusion.20), kind=kOutput, calls=%fused_computation.196 | output fusion | flops 12583039 | bytes 16843776 | tf_op jit(solution)/shard_map/sub | solution.py:56
  62.3 1.2 fusion.49
  63.5 0.8 convert_reduce_fusion
  64.3 0.5 fusion.28
  65.3 7.0 %fusion.33 = bf16[1024,512]{1,0:T(8,128)(2,1)S(1)} fusion(bf16[1024,512]{1,0:T(8,128)(2,1)} %copy-done.3, bf16[2048,512]{1,0:T(8,128)(2,1)S(1)} %copy-done, bf16[512,2048]{1,0:T(8,128)(2,1)} %param.14, f32[1024]{0:T(1024)S(1)} %add_rsqrt_fusion.1, f32[1024]{0:T(1024)S(1)} %broadcast_multiply_fusion.1), kind=kOutput, calls=%fused_computation.46 | convolution fusion | flops 4317511680 | bytes 6299648 | tf_op jit(solution)/shard_map/dot_general | solution.py:74
  72.3 2.4 %fusion.130 = (bf16[8,16,1,512]{3,2,1,0:T(2,128)(2,1)S(1)}, bf16[8,16,1,512]{3,2,1,0:T(2,128)(2,1)S(1)}, bf16[8,16,1,512]{3,2,1,0:T(2,128)(2,1)S(1)}, bf16[8,16,...) fusion(bf16[8,16,8,512]{3,2,1,0:T(8,128)(2,1)S(1)} %bitcast.181), kind=kLoop, calls=%fused_computation.195 | loop fusion | bytes 2097152 | tf_op jit(solution)/shard_map/split | solution.py:15
  74.7 0.7 fusion.95
  75.4 0.7 fusion.94
  76.1 0.7 fusion.93
  76.7 0.7 fusion.92
  77.4 0.7 fusion.91
  78.1 0.7 fusion.90
  78.7 0.7 fusion.89
  79.4 0.7 fusion.88
  80.1 4.3 %all-to-all-start.1 = ((bf16[8,8,16,1,512]{4,2,1,3,0:T(8,128)(2,1)}), bf16[8,8,16,1,512]{4,2,1,3,0:T(8,128)(2,1)S(1)}, u32[]{:S(2)}, u32[]{:S(2)}) async-start(bf16[8,8,16,1,512]{4,2,1,3,0:T(8,128)(2,1)} %fusion.88), calls=%async_computation.1 | async-start | bytes 2097152 | tf_op jit(solution)/shard_map/all_to_all | solution.py:14
  84.4 2.6 %copy.98 = bf16[512,1536]{0,1:T(8,128)(2,1)} copy(bf16[512,1536]{1,0:T(8,128)(2,1)} %param.16) | data formatting | bytes 3145728 | tf_op args[7]
  87.5 2.3 %fusion.128 = (bf16[512,1,16,32]{0,3,2,1:T(8,128)(2,1)S(1)}, bf16[512,1,16,32]{0,3,2,1:T(8,128)(2,1)S(1)}, bf16[512,1,16,32]{0,3,2,1:T(8,128)(2,1)}) fusion(bf16[512,3,16,32]{0,3,2,1:T(8,128)(2,1)} %bitcast.180), kind=kLoop, calls=%fused_computation.193 | loop fusion | bytes 3145728 | tf_op jit(solution)/shard_map/slice | solution.py:46
  89.8 10.5 %all-to-all-done.1 = bf16[8,8,16,1,512]{4,2,1,3,0:T(8,128)(2,1)S(1)} async-done(((bf16[8,8,16,1,512]{4,2,1,3,0:T(8,128)(2,1)}), bf16[8,8,16,1,512]{4,2,1,3,0:T(8,128)(2,1)S(1)}, u32[]{:S(2)}, u32[]{:S(2)}) %all-to-all-start.1) | async-done | bytes 1048608 | tf_op jit(solution)/shard_map/all_to_all | solution.py:14
  100.6 0.5 multiply_reduce_fusion
  101.6 0.6 copy-done.2
  102.2 0.7 fusion.133
  102.9 0.7 fusion.134
  103.7 0.7 fusion.135
  105.0 1.3 fusion.62
  106.3 3.5 %fusion.132 = (f32[16,8,128]{2,1,0:T(8,128)S(1)}, f32[16,8,128,128]{2,3,1,0:T(8,128)S(1)}) fusion(f32[16,8,128,128]{2,3,1,0:T(8,128)S(1)} %fusion.62, pred[8,128]{1,0:T(8,128)(4,1)S(1)} %broadcast_compare_fusion), kind=kOutput, calls=%fused_computation.197 | output fusion | flops 12583039 | bytes 16843776 | tf_op jit(solution)/shard_map/sub | solution.py:56
  109.8 1.2 fusion.50
  111.0 0.8 fusion.34
  111.8 0.6 copy.104
  112.4 18.4 %all_to_all.37 = bf16[8,128,1,512]{3,0,2,1:T(8,128)(2,1)S(1)} all-to-all(bf16[8,128,1,512]{3,0,2,1:T(8,128)(2,1)S(1)} %copy.104), channel_id=1, replica_groups=mesh['win'=32,'grp'=8] {'grp'}, dimensions={1} | all-to-all | bytes 2097152 | tf_op jit(solution)/shard_map/all_to_all | solution.py:173
  131.1 0.6 copy.106
  131.7 1.3 fusion.44
  133.0 33.5 %all_to_all.38 = bf16[32,32,512]{2,1,0:T(8,128)(2,1)S(1)} all-to-all(bf16[32,32,512]{2,1,0:T(8,128)(2,1)S(1)} %bitcast.194), channel_id=1, replica_groups=mesh['win'=32,'grp'=8] {'win'}, dimensions={0} | all-to-all | bytes 2097152 | tf_op jit(solution)/shard_map/all_to_all | solution.py:177
  166.5 1.6 fusion.52
  (50 shorter events, 4.0 us)
Async XLA Ops:
  0.0 65.3 %copy-start = (bf16[2048,512]{1,0:T(8,128)(2,1)S(1)}, bf16[2048,512]{1,0:T(8,128)(2,1)}, u32[]{:S(2)}) copy-start(bf16[2048,512]{1,0:T(8,128)(2,1)} %param.15) | copy-start | bytes 6291460
  6.8 45.3 %all-to-all-start = ((bf16[32,32,640]{2,1,0:T(8,128)(2,1)}), bf16[32,32,640]{2,1,0:T(8,128)(2,1)S(1)}, u32[]{:S(2)}, u32[]{:S(2)}) async-start(bf16[32,32,640]{2,1,0:T(8,128)(2,1)} %bitcast.191), calls=%async_computation | async-start | bytes 2621440 | tf_op jit(solution)/shard_map/all_to_all | solution.py:141
  18.1 2.6 %copy-start.7 = (s32[8,32,8]{1,2,0:T(8,128)S(1)}, s32[8,32,8]{1,2,0:T(8,128)}, u32[]{:S(2)}) copy-start(s32[8,32,8]{1,2,0:T(8,128)} %param.11) | copy-start | bytes 24580
  52.5 1.9 %copy-start.6 = (bf16[512,1,16,32]{0,3,2,1:T(8,128)(2,1)S(1)}, bf16[512,1,16,32]{0,3,2,1:T(8,128)(2,1)}, u32[]{:S(2)}) copy-start(bf16[512,1,16,32]{0,3,2,1:T(8,128)(2,1)} %get-tuple-element.9) | copy-start | bytes 1572868
  54.4 1.0 copy-start.5
  55.3 1.1 copy-start.4
  62.3 1.2 copy-start.8
  64.3 1.0 copy-start.3
  80.1 20.2 %all-to-all-start.1 = ((bf16[8,8,16,1,512]{4,2,1,3,0:T(8,128)(2,1)}), bf16[8,8,16,1,512]{4,2,1,3,0:T(8,128)(2,1)S(1)}, u32[]{:S(2)}, u32[]{:S(2)}) async-start(bf16[8,8,16,1,512]{4,2,1,3,0:T(8,128)(2,1)} %fusion.88), calls=%async_computation.1 | async-start | bytes 2097152 | tf_op jit(solution)/shard_map/all_to_all | solution.py:14
  101.1 1.0 copy-start.2
  109.8 1.2 copy-start.9
  133.0 35.1 %copy-start.1 = (bf16[2048,512]{1,0:T(8,128)(2,1)S(1)}, bf16[2048,512]{1,0:T(8,128)(2,1)}, u32[]{:S(2)}) copy-start(bf16[2048,512]{1,0:T(8,128)(2,1)} %param.15) | copy-start | bytes 6291460
